TPU v7x, 256 devices: a whole 4x4x8 slice. The times are simulated.
256 devices in a mesh: agent: 4 (over y), tile: 64 (over x, z, core).
Axes of the slice: x: 4, y: 4, z: 8, core: 2. Of those that a mesh axis runs over, the one named last changes fastest.
Arguments:
- feats: bfloat16 [32, 256, 24, 256], P('agent', 'tile'), may hold values from -18 to 18
- types: int32 [32], replicated, may hold values from 0 to 1
- valid: int32 [32], replicated, may hold values 0 or 1
- offsets: int32 [32, 2], replicated, may hold values from -2 to 2
- w_qkv: bfloat16 [2, 256, 768], replicated, may hold values from -0.375 to 0.375
- w_out: bfloat16 [2, 256, 256], replicated, may hold values from -0.375 to 0.375
- d_out: bfloat16 [32, 256, 24, 256], P('agent', 'tile'), may hold values from -6 to 6
Outputs:
- d_feats: bfloat16 [32, 256, 24, 256], P('agent', 'tile')
- g_qkv: float32 [2, 256, 768], P(None, 'tile')
- g_out: float32 [2, 256, 256], P(None, 'tile')
All inputs are finite; a program needn't handle non-finite values.
Results may differ from a plain program's by a relative error of at most 0.012.
The roundings to bfloat16 on the way count: a program that leaves them out, or rounds other values in their place, can miss the bound.
Values may be sent and summed in bfloat16 or wider, within the bound.
No kernel may reach another device: no remote copies, remote signals or barrier semaphores. Data moves between devices by JAX's collectives and lax.ppermute only.
A program may use at most 128 MiB of HBM per device.

v0:
```python
import math
import jax
import jax.numpy as jnp
from jax import lax
from jax.sharding import PartitionSpec as P

HEADS = 8
MAXOFF = 2


def axis_bits(axis):
    count = lax.axis_size(axis)
    bits = count.bit_length() - 1
    assert 1 << bits == count
    return bits


def xor_pairs(count, bit):
    return [(i, i ^ 1 << bit) for i in range(count)]


def tile_bit_order(count):
    bits = count.bit_length() - 1
    preferred = [0, 1, 4, 2, 5, 3]
    return [b for b in preferred if b < bits] + [b for b in range(bits) if b not in preferred]


def halving_sum(pieces, axis, bit_order):
    count = lax.axis_size(axis)
    me = lax.axis_index(axis)
    bits = axis_bits(axis)
    rest = pieces.shape[1:]
    x = pieces.reshape((2,) * bits + rest)
    for bit in bit_order:
        dim = bits - 1 - bit
        mine = me >> bit & 1
        low = lax.index_in_dim(x, 0, dim, keepdims=True)
        high = lax.index_in_dim(x, 1, dim, keepdims=True)
        keep = jnp.where(mine == 1, high, low)
        send = jnp.where(mine == 1, low, high)
        x = keep + lax.ppermute(send, axis, xor_pairs(count, bit))
    return x.reshape(rest)


def doubling_sum(x, axis, bit_order):
    count = lax.axis_size(axis)
    for bit in bit_order:
        x = x + lax.ppermute(x, axis, xor_pairs(count, bit))
    return x


def with_halo(cells, sides, width):
    for axis, dim in sides:
        count = lax.axis_size(axis)
        ends = count - 1
        head = lax.slice_in_dim(cells, 0, width, axis=dim)
        tail = lax.slice_in_dim(cells, cells.shape[dim] - width, cells.shape[dim], axis=dim)
        cells = jnp.concatenate(
            [
                lax.ppermute(tail, axis, [(i, (i + 1) % count) for i in range(ends)]),
                cells,
                lax.ppermute(head, axis, [((i + 1) % count, i) for i in range(ends)]),
            ],
            axis=dim,
        )
    return cells


def relocate(rimmed, offsets, direction):
    padded = jnp.pad(rimmed, ((0, 0), (0, 0), (MAXOFF, MAXOFF), (0, 0)))
    row_count = rimmed.shape[1] - 2 * MAXOFF
    col_count = rimmed.shape[2]

    def pick_one(plane, offset):
        row_start = MAXOFF + direction * offset[0]
        col_start = MAXOFF + direction * offset[1]
        return lax.dynamic_slice(
            plane, (row_start, col_start, jnp.int32(0)), (row_count, col_count, plane.shape[2])
        )

    return jax.vmap(pick_one)(padded, offsets)


def body(feats, types, valid, offsets, w_qkv, w_out, d_out):
    f32 = jnp.float32
    bf16 = jnp.bfloat16
    highest = lax.Precision.HIGHEST
    own_count, row_count, col_count, channels = feats.shape
    agents = own_count * lax.axis_size("agent")
    first_agent = lax.axis_index("agent") * own_count
    own_offsets = lax.dynamic_slice_in_dim(offsets, first_agent, own_count, 0)
    rimmed = with_halo(feats, (("tile", 1),), MAXOFF)
    warped = relocate(rimmed, own_offsets, 1)
    cell_count = row_count * col_count
    head_size = channels // HEADS
    score_scale = head_size ** (-0.5)
    all_hot = (types[:, None] == jnp.arange(2)[None, :]).astype(bf16)
    flat_feats = warped.reshape(own_count, cell_count, channels)
    flat_grads = d_out.reshape(own_count, cell_count, channels)
    all_feats, all_grads = (
        lax.all_to_all(flat_feats, "agent", split_axis=1, concat_axis=0, tiled=True),
        lax.all_to_all(flat_grads, "agent", split_axis=1, concat_axis=0, tiled=True),
    )
    part_cells = all_feats.shape[1]
    pairs = agents * part_cells
    is_type1 = (types == 1)[:, None, None]
    type_mask = jnp.stack([types == 0, types == 1], axis=0)[:, :, None, None]
    feats_rows = all_feats.reshape(pairs, channels)
    grads_rows = all_grads.reshape(pairs, channels)
    qkv_both = (
        jnp.einsum("pc,tce->tpe", feats_rows, w_qkv, preferred_element_type=f32)
        .astype(bf16)
        .reshape(2, agents, part_cells, 3 * channels)
    )
    qkv = jnp.where(is_type1, qkv_both[1], qkv_both[0])
    query_heads = qkv[..., :channels].reshape(agents, part_cells, HEADS, head_size)
    key_heads = qkv[..., channels : 2 * channels].reshape(agents, part_cells, HEADS, head_size)
    value_heads = qkv[..., 2 * channels :].reshape(agents, part_cells, HEADS, head_size)
    scores = (
        jnp.einsum("aghd,bghd->ghab", query_heads, key_heads, preferred_element_type=f32)
        * score_scale
    )
    agent_ids = jnp.arange(agents)
    allowed = (valid[None, :] == 1) | (agent_ids[:, None] == agent_ids[None, :])
    raised = jnp.where(allowed, jnp.exp(scores), f32(0.0))
    attn_prob = raised / jnp.sum(raised, axis=-1, keepdims=True)
    prob_low = attn_prob.astype(bf16)
    attended = (
        jnp.einsum("ghab,bghd->aghd", prob_low, value_heads, preferred_element_type=f32)
        .astype(bf16)
        .reshape(agents, part_cells, channels)
    )
    d_att_both = (
        jnp.einsum("pe,tce->tpc", grads_rows, w_out, preferred_element_type=f32)
        .astype(bf16)
        .reshape(2, agents, part_cells, channels)
    )
    d_attended = jnp.where(is_type1, d_att_both[1], d_att_both[0])
    attended_typed = jnp.where(type_mask, attended[None], jnp.zeros((), bf16))
    raw_out = jnp.einsum(
        "tpc,pe->tce",
        attended_typed.reshape(2, pairs, channels),
        grads_rows,
        preferred_element_type=f32,
    )
    attended_heads = d_attended.reshape(agents, part_cells, HEADS, head_size)
    prob_grad = jnp.einsum(
        "aghd,bghd->ghab", attended_heads, value_heads, preferred_element_type=f32
    )
    score_grad = (
        attn_prob
        * (prob_grad - jnp.sum(attn_prob * prob_grad, axis=-1, keepdims=True))
        * score_scale
    ).astype(bf16)
    d_query = (
        jnp.einsum("ghab,bghd->aghd", score_grad, key_heads, preferred_element_type=f32)
        .astype(bf16)
        .reshape(agents, part_cells, channels)
    )
    groups_n = agents // own_count
    grad_blocks = score_grad.reshape(part_cells, HEADS, groups_n, own_count, agents)
    prob_blocks = prob_low.reshape(part_cells, HEADS, groups_n, own_count, agents)
    query_blocks = query_heads.reshape(groups_n, own_count, part_cells, HEADS, head_size)
    dattn_blocks = attended_heads.reshape(groups_n, own_count, part_cells, HEADS, head_size)
    key_parts = jnp.einsum(
        "ghnyb,nyghd->nbghd", grad_blocks, query_blocks, preferred_element_type=f32
    ).astype(bf16)
    value_parts = jnp.einsum(
        "ghnyb,nyghd->nbghd", prob_blocks, dattn_blocks, preferred_element_type=f32
    ).astype(bf16)
    key_sum = jnp.sum(key_parts.astype(f32), axis=0).reshape(agents, part_cells, channels)
    value_sum = jnp.sum(value_parts.astype(f32), axis=0).reshape(agents, part_cells, channels)
    d_qkv = jnp.concatenate([d_query.astype(f32), key_sum, value_sum], axis=-1)
    d_hi = d_qkv.astype(bf16)
    d_lo = (d_qkv - d_hi.astype(f32)).astype(bf16)
    d_split = jnp.stack([d_hi, d_lo], axis=0).reshape(2, pairs, 3 * channels)
    d_part_terms = jnp.einsum("spe,tce->stpc", d_split, w_qkv, preferred_element_type=f32)
    d_part_sum = (d_part_terms[0] + d_part_terms[1]).reshape(2, agents, part_cells, channels)
    d_part = jnp.where(is_type1, d_part_sum[1], d_part_sum[0]).astype(bf16)
    returned = lax.all_to_all(d_part, "agent", split_axis=0, concat_axis=1, tiled=True)
    d_warped = returned.reshape(own_count, row_count, col_count, channels)
    feats_typed = jnp.where(type_mask, all_feats[None], jnp.zeros((), bf16)).reshape(
        2, pairs, channels
    )
    qkv_terms = jnp.einsum("tpc,spe->stce", feats_typed, d_split, preferred_element_type=f32)
    raw_qkv = qkv_terms[0] + qkv_terms[1]
    rimmed_grad = with_halo(d_warped, (("tile", 1),), MAXOFF)
    d_feats = relocate(rimmed_grad, own_offsets, -1)
    norm_limit = math.sqrt(8.0 * channels * channels)
    raw_all = jnp.concatenate([raw_qkv, raw_out], axis=-1)
    tiles = lax.axis_size("tile")
    share_rows = channels // tiles
    pieces = raw_all.reshape(2, tiles, share_rows, 4 * channels).transpose(1, 0, 2, 3)
    share_all = halving_sum(pieces, "tile", tile_bit_order(tiles))
    share_all = doubling_sum(share_all, "agent", list(range(axis_bits("agent"))))
    square_sum = jnp.broadcast_to(jnp.sum(share_all * share_all), (8, 128))
    square_sum = doubling_sum(square_sum, "tile", list(range(axis_bits("tile"))))[0, 0]
    factor = norm_limit / jnp.maximum(jnp.sqrt(square_sum), norm_limit)
    scaled = share_all * factor
    return (d_feats, scaled[..., : 3 * channels], scaled[..., 3 * channels :])


def solution(mesh):
    placed = (
        P("agent", "tile", None, None),
        P(),
        P(),
        P(),
        P(),
        P(),
        P("agent", "tile", None, None),
    )
    return jax.shard_map(
        body,
        mesh=mesh,
        in_specs=placed,
        out_specs=(P("agent", "tile", None, None), P(None, "tile", None), P(None, "tile", None)),
        check_vma=False,
    )
```

profile of v0, /device:TPU:2, one launch (start us, length us, event | category | flops | bytes accessed | tf_op | source)
XLA Modules:
  0.0 232.1 jit_solution(8492455447294959551)
XLA Ops:
  0.7 2.0 copy.109
  2.7 4.5 %all-to-all-start.1 = ((bf16[8,96,256]{2,0,1:T(8,128)(2,1)}), bf16[8,96,256]{2,0,1:T(8,128)(2,1)S(1)}, u32[]{:S(2)}, u32[]{:S(2)}) async-start(bf16[8,96,256]{2,0,1:T(8,128)(2,1)} %bitcast.10), calls=%async_computation.1 | async-start | bytes 786432 | tf_op jit(solution)/shard_map/all_to_all | solution.py:102
  7.2 1.2 copy.102
  8.4 1.9 collective-permute-start
  10.4 6.9 %collective-permute-start.1 = (bf16[8,2,24,256]{3,0,2,1:T(8,128)(2,1)S(1)}, bf16[8,2,24,256]{3,0,2,1:T(8,128)(2,1)S(1)}, u32[]{:S(2)}, u32[]{:S(2)}) collective-permute-start(bf16[8,2,24,256]{3,0,2,1:T(8,128)(2,1)S(1)} %get-tuple-element.33), channel_id=1, source_target_pairs={{1,0},{2,1},{3,2},{4,3},{5,4},{6,5},{7,6},{8,7},{9,8},{10,9},{11,1... | collective-permute-start | bytes 589832 | tf_op jit(solution)/shard_map/ppermute | solution.py:62
  18.7 1.8 collective-permute-done.1
  20.5 2.4 %gather_fusion = bf16[8,4,24,256]{3,0,2,1:T(8,128)(2,1)} fusion(bf16[8,8,28,256]{3,0,2,1:T(8,128)(2,1)S(1)} %fusion.32, s32[8]{0:T(128)S(1)} %get-tuple-element.35), kind=kCustom, calls=%fused_computation | custom fusion | bytes 786560 | tf_op jit(solution)/shard_map/vmap()/gather | solution.py:77
  23.0 5.0 %all-to-all-start = ((bf16[8,96,256]{2,0,1:T(8,128)(2,1)}), bf16[8,96,256]{2,0,1:T(8,128)(2,1)S(1)}, u32[]{:S(2)}, u32[]{:S(2)}) async-start(bf16[8,96,256]{2,0,1:T(8,128)(2,1)} %bitcast.1), calls=%async_computation | async-start | bytes 786432 | tf_op jit(solution)/shard_map/all_to_all | solution.py:101
  29.7 1.8 squeeze.33
  31.6 1.8 squeeze.36
  33.5 1.8 squeeze.34
  35.3 3.4 %broadcast_select_fusion = bf16[32,24,8,32]{3,2,1,0:T(8,128)(2,1)} fusion(bf16[32,24,8,32]{3,2,1,0:T(8,128)(2,1)} %squeeze.33, bf16[32,24,8,32]{3,2,1,0:T(8,128)(2,1)} %squeeze.34, pred[32]{0:T(512)(128)(4,1)S(1)} %get-tuple-element.38), kind=kLoop, calls=%fused_computation.44 | loop fusion | flops 196608 | bytes 1179680 | tf_op jit(solution)/shard_map/jit(_where)/select_n | solution.py:138
  38.7 1.4 broadcast_select_fusion.1
  41.4 1.8 reshape_reshape.4
  43.2 1.8 reshape.321
  45.0 1.6 copy.158
  47.6 3.8 %fusion.3 = (f32[24,8,32]{2,1,0:T(8,128)S(1)}, f32[24,8,32,32]{2,3,1,0:T(8,128)S(1)}) fusion(pred[32,32]{0,1:T(8,128)(4,1)S(1)} %fusion.44, bf16[32,24,8,32]{0,3,2,1:T(8,128)(2,1)S(1)} %bitcast.136, bf16[32,24,8,32]{3,2,1,0:T(8,128)(2,1)} %reshape.321), kind=kOutput, calls=%fused_computation.12 | convolution fusion | flops 13166592 | bytes 1598464 | tf_op jit(solution)/shard_map/aghd,bghd->ghab/dot_general | solution.py:120
  51.4 1.6 copy-done.5
  53.8 1.7 copy.125
  55.6 3.3 %fusion.26 = bf16[32,24,8,32]{0,3,2,1:T(8,128)(2,1)} fusion(bf16[32,24,8,32]{0,3,2,1:T(8,128)(2,1)} %bitcast.116, bf16[24,8,32,32]{2,3,1,0:T(8,128)(2,1)S(1)} %fusion.59), kind=kOutput, calls=%fused_computation.46 | convolution fusion | flops 12779520 | bytes 1179648 | tf_op jit(solution)/shard_map/ghab,bghd->aghd/dot_general | solution.py:129
  58.9 2.9 %fusion.22 = f32[24,8,32,32]{2,3,1,0:T(8,128)} fusion(bf16[32,24,8,32]{0,3,2,1:T(8,128)(2,1)S(1)} %bitcast.117, bf16[32,24,8,32]{3,2,1,0:T(8,128)(2,1)S(1)} %copy-done.3), kind=kOutput, calls=%fused_computation.40 | convolution fusion | flops 12582912 | bytes 1572864 | tf_op jit(solution)/shard_map/aghd,bghd->ghab/dot_general | solution.py:147
  61.8 8.2 %fusion.15 = f32[24,8,32,32]{3,2,1,0:T(8,128)} fusion(bf16[32,24,8,32]{0,3,2,1:T(8,128)(2,1)S(1)} %bitcast.137, f32[24,8,32,32]{2,3,1,0:T(8,128)} %fusion.22, f32[24,8,32,32]{2,3,1,0:T(8,128)} %copy-done.5, f32[24,8,32]{2,1,0:T(8,128)S(1)} %get-tuple-element.39, pred[32,32]{0,1:T(8,128)(4,1)S(1)} %fusion.44), kind=kOutput, calls=%fused_computation.31 | convolution fusion | flops 15144991 | bytes 2778112 | tf_op jit(solution)/shard_map/ghab,bghd->aghd/dot_general | solution.py:156
  70.0 6.7 %multiply_convert_fusion = bf16[24,8,32,32]{2,3,1,0:T(8,128)(2,1)S(1)} fusion(f32[24,8,32,32]{2,3,1,0:T(8,128)} %fusion.22, f32[24,8,32]{2,1,0:T(8,128)} %copy-done.16, f32[24,8,32,32]{2,3,1,0:T(8,128)} %copy-done.5, pred[32,32]{0,1:T(8,128)(4,1)S(1)} %fusion.44), kind=kOutput, calls=%fused_computation.5 | output fusion | flops 2168863 | bytes 1991680 | tf_op jit(solution)/shard_map/sub | solution.py:152
  76.8 4.5 %convert_reduce_fusion = f32[24,8,32,32]{3,2,1,0:T(8,128)} fusion(bf16[4,8,24,8,32]{4,3,2,1,0:T(8,128)(2,1)S(1)} %copy-done.7, bf16[24,8,32,32]{3,2,1,0:T(8,128)(2,1)S(1)} %copy-done.8), kind=kOutput, calls=%fused_computation.3 | convolution fusion | flops 14745600 | bytes 1572864 | tf_op jit(solution)/shard_map/ghnyb,nyghd->nbghd/dot_general | solution.py:168
  81.3 2.3 copy.152
  83.6 1.6 copy.119
  85.2 2.3 copy.132
  87.5 6.2 %convert_reduce_fusion.1 = f32[24,8,32,32]{3,2,1,0:T(8,128)} fusion(bf16[4,8,24,8,32]{4,3,2,1,0:T(8,128)(2,1)} %reshape_reshape.4, bf16[24,8,32,32]{3,2,1,0:T(8,128)(2,1)} %copy.119), kind=kOutput, calls=%fused_computation.4 | convolution fusion | flops 14745600 | bytes 1572864 | tf_op jit(solution)/shard_map/ghnyb,nyghd->nbghd/dot_general | solution.py:165
  93.7 2.3 copy.151
  96.0 1.2 subtract_convert_fusion
  99.3 3.8 %copy.137 = bf16[32,24,8,32]{3,2,1,0:T(8,128)(2,1)S(1)} copy(bf16[32,24,8,32]{0,3,2,1:T(8,128)(2,1)} %fusion.26) | data formatting | bytes 786432 | tf_op jit(solution)/shard_map/convert_element_type | solution.py:130
  103.0 1.8 broadcast_in_dim.106
  104.9 2.8 %fusion.12 = f32[2,2,256,768]{2,3,1,0:T(8,128)S(1)} fusion(bf16[1,32,24,768]{3,1,2,0:T(8,128)(2,1)S(1)} %copy-done.13, bf16[1,32,24,768]{3,1,2,0:T(8,128)(2,1)} %fusion.16, pred[2,32]{1,0:T(4,128)(4,1)S(1)} %copy-done.20, bf16[32,24,256]{2,0,1:T(8,128)(2,1)} %copy.134), kind=kOutput, calls=%fused_computation.26 | convolution fusion | flops 1213071360 | bytes 5898304 | tf_op jit(solution)/shard_map/tpc,spe->stce/dot_general | solution.py:185
  109.6 2.4 %copy.139 = f32[2,256,1024]{2,0,1:T(2,128)} copy(f32[2,256,1024]{1,2,0:T(8,128)S(1)} %pad_maximum_fusion.1) | data formatting | bytes 4194304 | tf_op jit(solution)/shard_map/concatenate | solution.py:190
  112.0 2.4 %fusion.62 = (f32[2,2,2,2,2,1,2,4,1024]{8,6,7,5,4,3,2,1,0:T(2,128)S(1)}, f32[2,2,2,2,2,1,2,4,1024]{8,6,7,5,4,3,2,1,0:T(2,128)S(1)}) fusion(f32[2,2,2,2,2,2,2,4,1024]{8,6,7,5,4,3,2,1,0:T(2,128)} %bitcast.124), kind=kLoop, calls=%fused_computation.114 | loop fusion | bytes 4194304 | tf_op jit(solution)/shard_map/slice | solution.py:38
  116.4 2.8 %collective-permute-done.4 = f32[2,2,2,2,2,1,2,4,1024]{8,7,6,5,4,3,2,1,0:T(4,128)} collective-permute-done((f32[2,2,2,2,2,1,2,4,1024]{8,7,6,5,4,3,2,1,0:T(4,128)S(1)}, f32[2,2,2,2,2,1,2,4,1024]{8,7,6,5,4,3,2,1,0:T(4,128)}, u32[]{:S(2)}, u32[]{:S(2)}) %collective-permute-start.4) | collective-permute-done | bytes 1048608 | tf_op jit(solution)/shard_map/ppermute | solution.py:41
  119.2 2.6 %select_add_fusion = f32[2,2,2,2,2,1,2,4,1024]{8,7,6,5,4,3,2,1,0:T(4,128)S(1)} fusion(f32[2,2,2,2,2,1,2,4,1024]{8,7,6,5,4,3,2,1,0:T(4,128)} %collective-permute-done.4, f32[2,2,2,2,2,1,2,4,1024]{8,6,7,5,4,3,2,1,0:T(2,128)} %copy-done.2, f32[2,2,2,2,2,1,2,4,1024]{8,6,7,5,4,3,2,1,0:T(2,128)S(1)} %get-tuple-element.21, pred[]{:T(512)S(6)} %eq.62), kind=kLoop, calls=%fused_computation.50 | loop fusion | flops 524288 | bytes 4194305 | tf_op jit(solution)/shard_map/add | solution.py:41
  123.2 5.2 %copy.118 = f32[32,24,8,32]{3,2,1,0:T(8,128)} copy(f32[32,24,8,32]{0,3,2,1:T(8,128)} %bitcast.121) | data formatting | bytes 1572864 | tf_op jit(solution)/shard_map/concatenate | solution.py:173
  128.4 2.4 %reshape.330 = f32[1,768,256]{2,1,0:T(8,128)S(1)} reshape(f32[32,24,8,32]{3,2,1,0:T(8,128)} %copy.118) | data formatting | bytes 1572864 | tf_op jit(solution)/shard_map/concatenate | solution.py:173
  130.8 4.8 %copy.122 = f32[32,24,8,32]{3,2,1,0:T(8,128)} copy(f32[32,24,8,32]{0,3,2,1:T(8,128)} %bitcast.123) | data formatting | bytes 1572864 | tf_op jit(solution)/shard_map/reduce_sum | solution.py:171
  135.6 2.4 %concatenate.75 = f32[1,768,256]{2,1,0:T(8,128)S(1)} reshape(f32[32,24,8,32]{3,2,1,0:T(8,128)} %copy.122) | data formatting | bytes 1572864 | tf_op jit(solution)/shard_map/concatenate | solution.py:173
  138.0 4.8 %copy.128 = f32[32,24,8,32]{3,2,1,0:T(8,128)} copy(f32[32,24,8,32]{0,3,2,1:T(8,128)} %bitcast.119) | data formatting | bytes 1572864 | tf_op jit(solution)/shard_map/reduce_sum | solution.py:172
  142.8 3.1 %concatenate.76 = f32[1,768,256]{2,1,0:T(8,128)} reshape(f32[32,24,8,32]{3,2,1,0:T(8,128)} %copy.128) | data formatting | bytes 1572864 | tf_op jit(solution)/shard_map/concatenate | solution.py:173
  147.1 1.3 select_add_fusion.1
  149.4 7.5 %collective-permute-done.6 = f32[2,1,2,2,1,1,2,4,1024]{8,7,6,5,4,3,2,1,0:T(4,128)S(1)} collective-permute-done((f32[2,1,2,2,1,1,2,4,1024]{8,7,6,5,4,3,2,1,0:T(4,128)S(1)}, f32[2,1,2,2,1,1,2,4,1024]{8,7,6,5,4,3,2,1,0:T(4,128)S(1)}, u32[]{:S(2)}, u32[]{:S(2)}) %collective-permute-start.6) | collective-permute-done | bytes 262176 | tf_op jit(solution)/shard_map/ppermute | solution.py:41
  157.0 5.8 %collective-permute-start.7 = (f32[2,1,2,1,1,1,2,4,1024]{8,7,6,5,4,3,2,1,0:T(4,128)S(1)}, f32[2,1,2,1,1,1,2,4,1024]{8,7,6,5,4,3,2,1,0:T(4,128)S(1)}, u32[]{:S(2)}, u32[]{:S(2)}) collective-permute-start(f32[2,1,2,1,1,1,2,4,1024]{8,7,6,5,4,3,2,1,0:T(4,128)S(1)} %slice_select_fusion.2), channel_id=1, source_target_pairs={{0,4},{1,5},{2,6},{3,7},{4,0},{5,1},{6,2},{7,3},{8,12},{9,13},{10,... | collective-permute-start | bytes 393224 | tf_op jit(solution)/shard_map/ppermute | solution.py:41
  162.8 1.4 fusion.13
  164.2 4.3 %collective-permute-done.7 = f32[2,1,2,1,1,1,2,4,1024]{8,7,6,5,4,3,2,1,0:T(4,128)S(1)} collective-permute-done((f32[2,1,2,1,1,1,2,4,1024]{8,7,6,5,4,3,2,1,0:T(4,128)S(1)}, f32[2,1,2,1,1,1,2,4,1024]{8,7,6,5,4,3,2,1,0:T(4,128)S(1)}, u32[]{:S(2)}, u32[]{:S(2)}) %collective-permute-start.7) | collective-permute-done | bytes 131104 | tf_op jit(solution)/shard_map/ppermute | solution.py:41
  168.6 2.2 collective-permute-start.8
  171.0 3.5 %collective-permute-done.8 = f32[1,1,2,1,1,1,2,4,1024]{8,7,6,5,4,3,2,1,0:T(4,128)S(1)} collective-permute-done((f32[1,1,2,1,1,1,2,4,1024]{8,7,6,5,4,3,2,1,0:T(4,128)S(1)}, f32[1,1,2,1,1,1,2,4,1024]{8,7,6,5,4,3,2,1,0:T(4,128)S(1)}, u32[]{:S(2)}, u32[]{:S(2)}) %collective-permute-start.8) | collective-permute-done | bytes 65568 | tf_op jit(solution)/shard_map/ppermute | solution.py:41
  174.5 2.4 %collective-permute-start.9 = (f32[1,1,1,1,1,1,2,4,1024]{8,7,6,5,4,3,2,1,0:T(4,128)S(1)}, f32[1,1,1,1,1,1,2,4,1024]{8,7,6,5,4,3,2,1,0:T(4,128)S(1)}, u32[]{:S(2)}, u32[]{:S(2)}) collective-permute-start(f32[1,1,1,1,1,1,2,4,1024]{8,7,6,5,4,3,2,1,0:T(4,128)S(1)} %slice_select_fusion.4), channel_id=1, source_target_pairs={{0,8},{1,9},{2,10},{3,11},{4,12},{5,13},{6,14},{7,15},{8,0},{9,1},... | collective-permute-start | bytes 98312 | tf_op jit(solution)/shard_map/ppermute | solution.py:41
  177.0 5.4 %collective-permute-done.9 = f32[1,1,1,1,1,1,2,4,1024]{8,7,6,5,4,3,2,1,0:T(4,128)S(1)} collective-permute-done((f32[1,1,1,1,1,1,2,4,1024]{8,7,6,5,4,3,2,1,0:T(4,128)S(1)}, f32[1,1,1,1,1,1,2,4,1024]{8,7,6,5,4,3,2,1,0:T(4,128)S(1)}, u32[]{:S(2)}, u32[]{:S(2)}) %collective-permute-start.9) | collective-permute-done | bytes 32800 | tf_op jit(solution)/shard_map/ppermute | solution.py:41
  182.4 1.8 collective-permute-start.10
  185.1 3.9 %all-to-all-start.2 = ((bf16[32,24,256]{2,1,0:T(8,128)(2,1)}), bf16[32,24,256]{2,1,0:T(8,128)(2,1)S(1)}, u32[]{:S(2)}, u32[]{:S(2)}) async-start(bf16[32,24,256]{2,1,0:T(8,128)(2,1)} %select_convert_fusion), calls=%async_computation.2 | async-start | bytes 786432 | tf_op jit(solution)/shard_map/all_to_all | solution.py:180
  189.1 3.6 %collective-permute-start.11 = (f32[2,4,1024]{2,1,0:T(4,128)S(1)}, f32[2,4,1024]{2,1,0:T(4,128)S(1)}, u32[]{:S(2)}, u32[]{:S(2)}) collective-permute-start(f32[2,4,1024]{2,1,0:T(4,128)S(1)} %add.123), channel_id=1, source_target_pairs={{0,128},{64,192},{128,0},{192,64},{1,129},{65,193},{129,1},{193,65... | collective-permute-start | bytes 98312 | tf_op jit(solution)/shard_map/ppermute | solution.py:48
  192.7 4.1 %collective-permute-done.11 = f32[2,4,1024]{2,1,0:T(4,128)S(1)} collective-permute-done((f32[2,4,1024]{2,1,0:T(4,128)S(1)}, f32[2,4,1024]{2,1,0:T(4,128)S(1)}, u32[]{:S(2)}, u32[]{:S(2)}) %collective-permute-start.11) | collective-permute-done | bytes 32800 | tf_op jit(solution)/shard_map/ppermute | solution.py:48
  200.3 2.1 collective-permute-start.2
  202.3 5.6 %collective-permute-start.3 = (bf16[8,2,24,256]{3,0,2,1:T(8,128)(2,1)S(1)}, bf16[8,2,24,256]{3,0,2,1:T(8,128)(2,1)S(1)}, u32[]{:S(2)}, u32[]{:S(2)}) collective-permute-start(bf16[8,2,24,256]{3,0,2,1:T(8,128)(2,1)S(1)} %get-tuple-element.31), channel_id=1, source_target_pairs={{1,0},{2,1},{3,2},{4,3},{5,4},{6,5},{7,6},{8,7},{9,8},{10,9},{11,1... | collective-permute-start | bytes 589832 | tf_op jit(solution)/shard_map/ppermute | solution.py:62
  209.8 3.4 %collective-permute-done.14 = f32[8,128]{1,0:T(8,128)S(1)} collective-permute-done((f32[8,128]{1,0:T(8,128)S(1)}, f32[8,128]{1,0:T(8,128)S(1)}, u32[]{:S(2)}, u32[]{:S(2)}) %collective-permute-start.14) | collective-permute-done | bytes 4128 | tf_op jit(solution)/shard_map/ppermute | solution.py:48
  213.2 1.4 collective-permute-start.15
  214.7 6.1 %collective-permute-done.15 = f32[8,128]{1,0:T(8,128)S(1)} collective-permute-done((f32[8,128]{1,0:T(8,128)S(1)}, f32[8,128]{1,0:T(8,128)S(1)}, u32[]{:S(2)}, u32[]{:S(2)}) %collective-permute-start.15) | collective-permute-done | bytes 4128 | tf_op jit(solution)/shard_map/ppermute | solution.py:48
  220.9 3.5 %collective-permute-done.16 = f32[8,128]{1,0:T(8,128)S(1)} collective-permute-done((f32[8,128]{1,0:T(8,128)S(1)}, f32[8,128]{1,0:T(8,128)S(1)}, u32[]{:S(2)}, u32[]{:S(2)}) %collective-permute-start.16) | collective-permute-done | bytes 4128 | tf_op jit(solution)/shard_map/ppermute | solution.py:48
  224.4 2.1 collective-permute-start.17
  226.6 1.7 gather_fusion.1
  (126 shorter events, 25.5 us)
Async XLA Ops:
  0.6 39.5 %copy-start = (bf16[2,256,768]{2,1,0:T(8,128)(2,1)S(1)}, bf16[2,256,768]{2,1,0:T(8,128)(2,1)}, u32[]{:S(2)}) copy-start(bf16[2,256,768]{2,1,0:T(8,128)(2,1)} %param.11) | copy-start | bytes 2359300
  0.6 16.6 %copy-start.22 = (s32[32]{0:T(128)S(1)}, s32[32]{0:T(128)}, u32[]{:S(2)}) copy-start(s32[32]{0:T(128)} %param.9) | copy-start | bytes 388
  0.7 16.6 %copy-start.21 = (s32[32]{0:T(128)S(1)}, s32[32]{0:T(128)}, u32[]{:S(2)}) copy-start(s32[32]{0:T(128)} %param.8) | copy-start | bytes 388
  0.7 17.5 %copy-start.17 = (s32[32,2]{0,1:T(2,128)S(1)}, s32[32,2]{0,1:T(2,128)}, u32[]{:S(2)}) copy-start(s32[32,2]{0,1:T(2,128)} %param.10) | copy-start | bytes 772
  2.7 20.2 %all-to-all-start.1 = ((bf16[8,96,256]{2,0,1:T(8,128)(2,1)}), bf16[8,96,256]{2,0,1:T(8,128)(2,1)S(1)}, u32[]{:S(2)}, u32[]{:S(2)}) async-start(bf16[8,96,256]{2,0,1:T(8,128)(2,1)} %bitcast.10), calls=%async_computation.1 | async-start | bytes 786432 | tf_op jit(solution)/shard_map/all_to_all | solution.py:102
  8.4 10.2 %collective-permute-start = (bf16[8,2,24,256]{3,0,2,1:T(8,128)(2,1)S(1)}, bf16[8,2,24,256]{3,0,2,1:T(8,128)(2,1)S(1)}, u32[]{:S(2)}, u32[]{:S(2)}) collective-permute-start(bf16[8,2,24,256]{3,0,2,1:T(8,128)(2,1)S(1)} %get-tuple-element.32), channel_id=1, source_target_pairs={{0,1},{1,2},{2,3},{3,4},{4,5},{5,6},{6,7},{7,8},{8,9},{9,10},{10,1... | collective-permute-start | bytes 589832 | tf_op jit(solution)/shard_map/ppermute | solution.py:60
  10.4 10.1 %collective-permute-start.1 = (bf16[8,2,24,256]{3,0,2,1:T(8,128)(2,1)S(1)}, bf16[8,2,24,256]{3,0,2,1:T(8,128)(2,1)S(1)}, u32[]{:S(2)}, u32[]{:S(2)}) collective-permute-start(bf16[8,2,24,256]{3,0,2,1:T(8,128)(2,1)S(1)} %get-tuple-element.33), channel_id=1, source_target_pairs={{1,0},{2,1},{3,2},{4,3},{5,4},{6,5},{7,6},{8,7},{9,8},{10,9},{11,1... | collective-permute-start | bytes 589832 | tf_op jit(solution)/shard_map/ppermute | solution.py:62
  18.0 0.7 copy-start.19
  20.5 7.6 %copy-start.15 = (bf16[2,256,256]{2,1,0:T(8,128)(2,1)S(1)}, bf16[2,256,256]{2,1,0:T(8,128)(2,1)}, u32[]{:S(2)}) copy-start(bf16[2,256,256]{2,1,0:T(8,128)(2,1)} %param.12) | copy-start | bytes 786436
  23.0 17.1 %all-to-all-start = ((bf16[8,96,256]{2,0,1:T(8,128)(2,1)}), bf16[8,96,256]{2,0,1:T(8,128)(2,1)S(1)}, u32[]{:S(2)}, u32[]{:S(2)}) async-start(bf16[8,96,256]{2,0,1:T(8,128)(2,1)} %bitcast.1), calls=%async_computation | async-start | bytes 786432 | tf_op jit(solution)/shard_map/all_to_all | solution.py:101
  28.1 0.8 copy-start.9
  35.2 3.4 %copy-start.4 = (bf16[4,8,24,8,32]{4,3,2,1,0:T(8,128)(2,1)S(1)}, bf16[4,8,24,8,32]{4,3,2,1,0:T(8,128)(2,1)}, u32[]{:S(2)}) copy-start(bf16[4,8,24,8,32]{4,3,2,1,0:T(8,128)(2,1)} %squeeze.36) | copy-start | bytes 1179652
  35.2 3.4 %copy-start.18 = (pred[4,8]{1,0:T(4,128)(4,1)S(1)}, pred[4,8]{1,0:T(4,128)(4,1)}, u32[]{:S(2)}) copy-start(pred[4,8]{1,0:T(4,128)(4,1)} %broadcast_in_dim.97) | copy-start | bytes 100
  47.5 3.8 %copy-start.11 = (bf16[32,24,256]{0,2,1:T(8,128)(2,1)}, bf16[32,24,256]{0,2,1:T(8,128)(2,1)S(1)}, u32[]{:S(2)}) copy-start(bf16[32,24,256]{0,2,1:T(8,128)(2,1)S(1)} %copy.157) | copy-start | bytes 1179652
  51.4 1.6 copy-start.5
  51.4 10.4 %copy-start.16 = (f32[24,8,32]{2,1,0:T(8,128)}, f32[24,8,32]{2,1,0:T(8,128)S(1)}, u32[]{:S(2)}) copy-start(f32[24,8,32]{2,1,0:T(8,128)S(1)} %get-tuple-element.39) | copy-start | bytes 73732
  55.6 3.3 %copy-start.1 = (bf16[32,24,256]{0,2,1:T(8,128)(2,1)S(1)}, bf16[32,24,256]{0,2,1:T(8,128)(2,1)}, u32[]{:S(2)}) copy-start(bf16[32,24,256]{0,2,1:T(8,128)(2,1)} %copy.158) | copy-start | bytes 1179652
  55.6 3.3 %copy-start.3 = (bf16[32,24,8,32]{3,2,1,0:T(8,128)(2,1)S(1)}, bf16[32,24,8,32]{3,2,1,0:T(8,128)(2,1)}, u32[]{:S(2)}) copy-start(bf16[32,24,8,32]{3,2,1,0:T(8,128)(2,1)} %broadcast_select_fusion) | copy-start | bytes 1179652
  58.9 2.9 %copy-start.12 = (bf16[32,24,256]{0,2,1:T(8,128)(2,1)S(1)}, bf16[32,24,256]{0,2,1:T(8,128)(2,1)}, u32[]{:S(2)}) copy-start(bf16[32,24,256]{0,2,1:T(8,128)(2,1)} %copy-done.11) | copy-start | bytes 1179652
  70.0 6.7 %copy-start.7 = (bf16[4,8,24,8,32]{4,3,2,1,0:T(8,128)(2,1)S(1)}, bf16[4,8,24,8,32]{4,3,2,1,0:T(8,128)(2,1)}, u32[]{:S(2)}) copy-start(bf16[4,8,24,8,32]{4,3,2,1,0:T(8,128)(2,1)} %broadcast_select_fusion.1) | copy-start | bytes 1179652
  70.0 6.7 %copy-start.8 = (bf16[24,8,32,32]{3,2,1,0:T(8,128)(2,1)S(1)}, bf16[24,8,32,32]{3,2,1,0:T(8,128)(2,1)}, u32[]{:S(2)}) copy-start(bf16[24,8,32,32]{3,2,1,0:T(8,128)(2,1)} %copy.125) | copy-start | bytes 1179652
  99.2 5.7 %copy-start.13 = (bf16[1,32,24,768]{3,1,2,0:T(8,128)(2,1)S(1)}, bf16[1,32,24,768]{3,1,2,0:T(8,128)(2,1)}, u32[]{:S(2)}) copy-start(bf16[1,32,24,768]{3,1,2,0:T(8,128)(2,1)} %subtract_convert_fusion) | copy-start | bytes 3538948
  99.3 5.7 %copy-start.20 = (pred[2,32]{1,0:T(4,128)(4,1)S(1)}, pred[2,32]{1,0:T(4,128)(4,1)}, u32[]{:S(2)}) copy-start(pred[2,32]{1,0:T(4,128)(4,1)} %copy-done.19) | copy-start | bytes 196
  107.7 1.0 copy-start.10
  107.8 1.1 copy-start.14
  114.4 1.0 copy-start.2
  116.3 2.9 %collective-permute-start.4 = (f32[2,2,2,2,2,1,2,4,1024]{8,7,6,5,4,3,2,1,0:T(4,128)S(1)}, f32[2,2,2,2,2,1,2,4,1024]{8,7,6,5,4,3,2,1,0:T(4,128)}, u32[]{:S(2)}, u32[]{:S(2)}) collective-permute-start(f32[2,2,2,2,2,1,2,4,1024]{8,7,6,5,4,3,2,1,0:T(4,128)S(1)} %copy_select_fusion), channel_id=1, source_target_pairs={{0,1},{1,0},{2,3},{3,2},{4,5},{5,4},{6,7},{7,6},{8,9},{9,8},{10,11... | collective-permute-start | bytes 3145736 | tf_op jit(solution)/shard_map/ppermute | solution.py:41
  122.7 24.3 %collective-permute-start.5 = (f32[2,2,2,2,1,1,2,4,1024]{8,7,6,5,4,3,2,1,0:T(4,128)}, f32[2,2,2,2,1,1,2,4,1024]{8,7,6,5,4,3,2,1,0:T(4,128)}, u32[]{:S(2)}, u32[]{:S(2)}) collective-permute-start(f32[2,2,2,2,1,1,2,4,1024]{8,7,6,5,4,3,2,1,0:T(4,128)} %slice_select_fusion), channel_id=1, source_target_pairs={{0,2},{1,3},{2,0},{3,1},{4,6},{5,7},{6,4},{7,5},{8,10},{9,11},{10,... | collective-permute-start | bytes 1572872 | tf_op jit(solution)/shard_map/ppermute | solution.py:41
  145.9 1.1 copy-start.6
  148.5 8.4 %collective-permute-start.6 = (f32[2,1,2,2,1,1,2,4,1024]{8,7,6,5,4,3,2,1,0:T(4,128)S(1)}, f32[2,1,2,2,1,1,2,4,1024]{8,7,6,5,4,3,2,1,0:T(4,128)S(1)}, u32[]{:S(2)}, u32[]{:S(2)}) collective-permute-start(f32[2,1,2,2,1,1,2,4,1024]{8,7,6,5,4,3,2,1,0:T(4,128)S(1)} %slice_select_fusion.1), channel_id=1, source_target_pairs={{0,16},{1,17},{2,18},{3,19},{4,20},{5,21},{6,22},{7,23},{8,24},{9,... | collective-permute-start | bytes 786440 | tf_op jit(solution)/shard_map/ppermute | solution.py:41
  157.0 11.5 %collective-permute-start.7 = (f32[2,1,2,1,1,1,2,4,1024]{8,7,6,5,4,3,2,1,0:T(4,128)S(1)}, f32[2,1,2,1,1,1,2,4,1024]{8,7,6,5,4,3,2,1,0:T(4,128)S(1)}, u32[]{:S(2)}, u32[]{:S(2)}) collective-permute-start(f32[2,1,2,1,1,1,2,4,1024]{8,7,6,5,4,3,2,1,0:T(4,128)S(1)} %slice_select_fusion.2), channel_id=1, source_target_pairs={{0,4},{1,5},{2,6},{3,7},{4,0},{5,1},{6,2},{7,3},{8,12},{9,13},{10,... | collective-permute-start | bytes 393224 | tf_op jit(solution)/shard_map/ppermute | solution.py:41
  168.6 5.9 %collective-permute-start.8 = (f32[1,1,2,1,1,1,2,4,1024]{8,7,6,5,4,3,2,1,0:T(4,128)S(1)}, f32[1,1,2,1,1,1,2,4,1024]{8,7,6,5,4,3,2,1,0:T(4,128)S(1)}, u32[]{:S(2)}, u32[]{:S(2)}) collective-permute-start(f32[1,1,2,1,1,1,2,4,1024]{8,7,6,5,4,3,2,1,0:T(4,128)S(1)} %slice_select_fusion.3), channel_id=1, source_target_pairs={{0,32},{1,33},{2,34},{3,35},{4,36},{5,37},{6,38},{7,39},{8,40},{9,... | collective-permute-start | bytes 196616 | tf_op jit(solution)/shard_map/ppermute | solution.py:41
  174.5 7.9 %collective-permute-start.9 = (f32[1,1,1,1,1,1,2,4,1024]{8,7,6,5,4,3,2,1,0:T(4,128)S(1)}, f32[1,1,1,1,1,1,2,4,1024]{8,7,6,5,4,3,2,1,0:T(4,128)S(1)}, u32[]{:S(2)}, u32[]{:S(2)}) collective-permute-start(f32[1,1,1,1,1,1,2,4,1024]{8,7,6,5,4,3,2,1,0:T(4,128)S(1)} %slice_select_fusion.4), channel_id=1, source_target_pairs={{0,8},{1,9},{2,10},{3,11},{4,12},{5,13},{6,14},{7,15},{8,0},{9,1},... | collective-permute-start | bytes 98312 | tf_op jit(solution)/shard_map/ppermute | solution.py:41
  182.4 6.6 %collective-permute-start.10 = (f32[2,4,1024]{2,1,0:T(4,128)S(1)}, f32[2,4,1024]{2,1,0:T(4,128)S(1)}, u32[]{:S(2)}, u32[]{:S(2)}) collective-permute-start(f32[2,4,1024]{2,1,0:T(4,128)S(1)} %add_bitcast_fusion), channel_id=1, source_target_pairs={{0,64},{64,0},{128,192},{192,128},{1,65},{65,1},{129,193},{193,129... | collective-permute-start | bytes 98312 | tf_op jit(solution)/shard_map/ppermute | solution.py:48
  185.1 13.2 %all-to-all-start.2 = ((bf16[32,24,256]{2,1,0:T(8,128)(2,1)}), bf16[32,24,256]{2,1,0:T(8,128)(2,1)S(1)}, u32[]{:S(2)}, u32[]{:S(2)}) async-start(bf16[32,24,256]{2,1,0:T(8,128)(2,1)} %select_convert_fusion), calls=%async_computation.2 | async-start | bytes 786432 | tf_op jit(solution)/shard_map/all_to_all | solution.py:180
  189.1 7.7 %collective-permute-start.11 = (f32[2,4,1024]{2,1,0:T(4,128)S(1)}, f32[2,4,1024]{2,1,0:T(4,128)S(1)}, u32[]{:S(2)}, u32[]{:S(2)}) collective-permute-start(f32[2,4,1024]{2,1,0:T(4,128)S(1)} %add.123), channel_id=1, source_target_pairs={{0,128},{64,192},{128,0},{192,64},{1,129},{65,193},{129,1},{193,65... | collective-permute-start | bytes 98312 | tf_op jit(solution)/shard_map/ppermute | solution.py:48
  198.0 1.4 collective-permute-start.12
  200.1 7.8 %collective-permute-start.13 = (f32[8,128]{1,0:T(8,128)S(1)}, f32[8,128]{1,0:T(8,128)S(1)}, u32[]{:S(2)}, u32[]{:S(2)}) collective-permute-start(f32[8,128]{1,0:T(8,128)S(1)} %broadcast_add_fusion), channel_id=1, source_target_pairs={{0,2},{1,3},{2,0},{3,1},{4,6},{5,7},{6,4},{7,5},{8,10},{9,11},{10,... | collective-permute-start | bytes 12296 | tf_op jit(solution)/shard_map/ppermute | solution.py:48
  200.3 26.2 %collective-permute-start.2 = (bf16[8,2,24,256]{3,0,2,1:T(8,128)(2,1)S(1)}, bf16[8,2,24,256]{3,0,2,1:T(8,128)(2,1)S(1)}, u32[]{:S(2)}, u32[]{:S(2)}) collective-permute-start(bf16[8,2,24,256]{3,0,2,1:T(8,128)(2,1)S(1)} %get-tuple-element.30), channel_id=1, source_target_pairs={{0,1},{1,2},{2,3},{3,4},{4,5},{5,6},{6,7},{7,8},{8,9},{9,10},{10,1... | collective-permute-start | bytes 589832 | tf_op jit(solution)/shard_map/ppermute | solution.py:60
  202.3 24.1 %collective-permute-start.3 = (bf16[8,2,24,256]{3,0,2,1:T(8,128)(2,1)S(1)}, bf16[8,2,24,256]{3,0,2,1:T(8,128)(2,1)S(1)}, u32[]{:S(2)}, u32[]{:S(2)}) collective-permute-start(bf16[8,2,24,256]{3,0,2,1:T(8,128)(2,1)S(1)} %get-tuple-element.31), channel_id=1, source_target_pairs={{1,0},{2,1},{3,2},{4,3},{5,4},{6,5},{7,6},{8,7},{9,8},{10,9},{11,1... | collective-permute-start | bytes 589832 | tf_op jit(solution)/shard_map/ppermute | solution.py:62
  208.6 4.6 %collective-permute-start.14 = (f32[8,128]{1,0:T(8,128)S(1)}, f32[8,128]{1,0:T(8,128)S(1)}, u32[]{:S(2)}, u32[]{:S(2)}) collective-permute-start(f32[8,128]{1,0:T(8,128)S(1)} %fusion.78), channel_id=1, source_target_pairs={{0,4},{1,5},{2,6},{3,7},{4,0},{5,1},{6,2},{7,3},{8,12},{9,13},{10,... | collective-permute-start | bytes 12296 | tf_op jit(solution)/shard_map/ppermute | solution.py:48
  213.2 7.5 %collective-permute-start.15 = (f32[8,128]{1,0:T(8,128)S(1)}, f32[8,128]{1,0:T(8,128)S(1)}, u32[]{:S(2)}, u32[]{:S(2)}) collective-permute-start(f32[8,128]{1,0:T(8,128)S(1)} %add.127), channel_id=1, source_target_pairs={{0,8},{1,9},{2,10},{3,11},{4,12},{5,13},{6,14},{7,15},{8,0},{9,1},... | collective-permute-start | bytes 12296 | tf_op jit(solution)/shard_map/ppermute | solution.py:48
  220.7 3.6 %collective-permute-start.16 = (f32[8,128]{1,0:T(8,128)S(1)}, f32[8,128]{1,0:T(8,128)S(1)}, u32[]{:S(2)}, u32[]{:S(2)}) collective-permute-start(f32[8,128]{1,0:T(8,128)S(1)} %add.128), channel_id=1, source_target_pairs={{0,16},{1,17},{2,18},{3,19},{4,20},{5,21},{6,22},{7,23},{8,24},{9,... | collective-permute-start | bytes 12296 | tf_op jit(solution)/shard_map/ppermute | solution.py:48
  224.4 5.1 %collective-permute-start.17 = (f32[8,128]{1,0:T(8,128)S(1)}, f32[8,128]{1,0:T(8,128)S(1)}, u32[]{:S(2)}, u32[]{:S(2)}) collective-permute-start(f32[8,128]{1,0:T(8,128)S(1)} %add.129), channel_id=1, source_target_pairs={{0,32},{1,33},{2,34},{3,35},{4,36},{5,37},{6,38},{7,39},{8,40},{9,... | collective-permute-start | bytes 12296 | tf_op jit(solution)/shard_map/ppermute | solution.py:48
where the time goes:
time: 235 us; the launch traced here: 232 us
  local copies, waits for them, and re-layouts  73.7 us (31%)
  starting transfers between devices  52.2 us (22%)
  waiting for transfers between devices  44.1 us (19%)
  matrix products  34.9 us (15%)
  other arithmetic  24.9 us (11%)
    ppermute x6, waiting for transfers between devices, halving_sum(): x = keep + lax.ppermute(send, axis, xor_pairs(count, bit))  23.5 us
    concatenate x8, local copies, waits for them, and re-layouts, body(): d_qkv = jnp.concatenate([d_query.astype(f32), key_sum, value_sum], axis=-1)  20.1 us
    ppermute x8, waiting for transfers between devices, doubling_sum(): x = x + lax.ppermute(x, axis, xor_pairs(count, bit))  18.5 us
    ppermute x2, starting transfers between devices, with_halo(): lax.ppermute(head, axis, [((i + 1) % count, i) for i in range(ends)])  12.5 us
    ppermute x6, starting transfers between devices, halving_sum(): x = keep + lax.ppermute(send, axis, xor_pairs(count, bit))  11.6 us
    ppermute x8, starting transfers between devices, doubling_sum(): x = x + lax.ppermute(x, axis, xor_pairs(count, bit))  10.7 us
    unnamed x51, local copies, waits for them, and re-layouts  9 us
    dot_general x1, matrix products, body(): jnp.einsum('ghab,bghd->aghd', score_grad, key_heads, preferred_element_ty...  8.25 us
  transfers between devices with their start and end apart: 21, of which 13 were waited for; matrix products, arithmetic and copies ran while one was open for 20% of the time, Pallas kernels for 0%

commit v1 on v0

--- a/solution.py
+++ b/solution.py
@@ -98,7 +98,12 @@
     flat_feats = warped.reshape(own_count, cell_count, channels)
     flat_grads = d_out.reshape(own_count, cell_count, channels)
     all_feats, all_grads = (
-        lax.all_to_all(flat_feats, "agent", split_axis=1, concat_axis=0, tiled=True),
+        jnp.concatenate(
+            lax.all_to_all(
+                jnp.stack(jnp.split(flat_feats, lax.axis_size("agent"), axis=1)), "agent", 0, 0
+            ),
+            axis=0,
+        ),
         lax.all_to_all(flat_grads, "agent", split_axis=1, concat_axis=0, tiled=True),
     )
     part_cells = all_feats.shape[1]

time: 235 us -> 236 us (level)
    unnamed x51 -> x53, local copies, waits for them, and re-layouts: 9 us -> 8.76 us
where the time goes in v1:
time: 236 us; the launch traced here: 233 us
  local copies, waits for them, and re-layouts  73.5 us (31%)
  starting transfers between devices  52.2 us (22%)
  waiting for transfers between devices  44.1 us (19%)
  matrix products  35 us (15%)
  other arithmetic  25.7 us (11%)
    ppermute x6, waiting for transfers between devices, halving_sum(): x = keep + lax.ppermute(send, axis, xor_pairs(count, bit))  23.4 us
    concatenate x8, local copies, waits for them, and re-layouts, body(): d_qkv = jnp.concatenate([d_query.astype(f32), key_sum, value_sum], axis=-1)  20.1 us
    ppermute x8, waiting for transfers between devices, doubling_sum(): x = x + lax.ppermute(x, axis, xor_pairs(count, bit))  18.5 us
    ppermute x2, starting transfers between devices, with_halo(): lax.ppermute(head, axis, [((i + 1) % count, i) for i in range(ends)])  12.5 us
    ppermute x6, starting transfers between devices, halving_sum(): x = keep + lax.ppermute(send, axis, xor_pairs(count, bit))  11.6 us
    ppermute x8, starting transfers between devices, doubling_sum(): x = x + lax.ppermute(x, axis, xor_pairs(count, bit))  10.7 us
    unnamed x53, local copies, waits for them, and re-layouts  8.76 us
    dot_general x1, matrix products, body(): jnp.einsum('ghab,bghd->aghd', score_grad, key_heads, preferred_element_ty...  8.23 us
  transfers between devices with their start and end apart: 21, of which 13 were waited for; matrix products, arithmetic and copies ran while one was open for 20% of the time, Pallas kernels for 0%

profile of v1, /device:TPU:2, one launch (start us, length us, event | category | flops | bytes accessed | tf_op | source)
XLA Modules:
  0.0 232.8 jit_solution(6998658115844097407)
XLA Ops:
  0.7 2.0 copy.81
  2.7 4.5 %all-to-all-start.1 = ((bf16[8,96,256]{2,0,1:T(8,128)(2,1)}), bf16[8,96,256]{2,0,1:T(8,128)(2,1)S(1)}, u32[]{:S(2)}, u32[]{:S(2)}) async-start(bf16[8,96,256]{2,0,1:T(8,128)(2,1)} %bitcast.11), calls=%async_computation.1 | async-start | bytes 786432 | tf_op jit(solution)/shard_map/all_to_all | solution.py:107
  7.2 1.2 copy.72
  8.4 1.9 collective-permute-start
  10.3 6.9 %collective-permute-start.1 = (bf16[8,2,24,256]{3,0,2,1:T(8,128)(2,1)S(1)}, bf16[8,2,24,256]{3,0,2,1:T(8,128)(2,1)S(1)}, u32[]{:S(2)}, u32[]{:S(2)}) collective-permute-start(bf16[8,2,24,256]{3,0,2,1:T(8,128)(2,1)S(1)} %get-tuple-element.34), channel_id=1, source_target_pairs={{1,0},{2,1},{3,2},{4,3},{5,4},{6,5},{7,6},{8,7},{9,8},{10,9},{11,1... | collective-permute-start | bytes 589832 | tf_op jit(solution)/shard_map/ppermute | solution.py:62
  18.7 1.8 collective-permute-done.1
  20.5 1.7 gather_fusion
  23.1 5.0 %all-to-all-start = ((bf16[4,8,24,256]{3,2,1,0:T(8,128)(2,1)}), bf16[4,8,24,256]{3,2,1,0:T(8,128)(2,1)S(1)}, u32[]{:S(2)}, u32[]{:S(2)}) async-start(bf16[4,8,24,256]{3,2,1,0:T(8,128)(2,1)} %pad_maximum_fusion.2), calls=%async_computation | async-start | bytes 786432 | tf_op jit(solution)/shard_map/all_to_all | solution.py:102
  30.3 1.8 squeeze.33
  32.3 1.8 squeeze.36
  34.1 1.8 squeeze.34
  35.9 3.4 %broadcast_select_fusion = bf16[32,24,8,32]{3,2,1,0:T(8,128)(2,1)} fusion(bf16[32,24,8,32]{3,2,1,0:T(8,128)(2,1)} %squeeze.33, bf16[32,24,8,32]{3,2,1,0:T(8,128)(2,1)} %squeeze.34, pred[32]{0:T(512)(128)(4,1)S(1)} %get-tuple-element.39), kind=kLoop, calls=%fused_computation.44 | loop fusion | flops 196608 | bytes 1179680 | tf_op jit(solution)/shard_map/jit(_where)/select_n | solution.py:143
  39.3 1.5 broadcast_select_fusion.1
  42.0 1.8 reshape_reshape.8
  43.8 1.8 reshape.315
  45.6 1.6 copy.131
  48.2 3.8 %fusion.3 = (f32[24,8,32]{2,1,0:T(8,128)S(1)}, f32[24,8,32,32]{2,3,1,0:T(8,128)S(1)}) fusion(pred[32,32]{0,1:T(8,128)(4,1)S(1)} %fusion.44, bf16[32,24,8,32]{0,3,2,1:T(8,128)(2,1)S(1)} %bitcast.138, bf16[32,24,8,32]{3,2,1,0:T(8,128)(2,1)} %reshape.315), kind=kOutput, calls=%fused_computation.12 | convolution fusion | flops 13166592 | bytes 1598464 | tf_op jit(solution)/shard_map/aghd,bghd->ghab/dot_general | solution.py:125
  52.0 1.6 copy-done.5
  54.5 1.8 copy.97
  56.2 3.3 %fusion.26 = bf16[32,24,8,32]{0,3,2,1:T(8,128)(2,1)} fusion(bf16[32,24,8,32]{0,3,2,1:T(8,128)(2,1)} %bitcast.119, bf16[24,8,32,32]{2,3,1,0:T(8,128)(2,1)S(1)} %fusion.59), kind=kOutput, calls=%fused_computation.46 | convolution fusion | flops 12779520 | bytes 1179648 | tf_op jit(solution)/shard_map/ghab,bghd->aghd/dot_general | solution.py:134
  59.6 2.9 %fusion.22 = f32[24,8,32,32]{2,3,1,0:T(8,128)} fusion(bf16[32,24,8,32]{0,3,2,1:T(8,128)(2,1)S(1)} %bitcast.120, bf16[32,24,8,32]{3,2,1,0:T(8,128)(2,1)S(1)} %copy-done.3), kind=kOutput, calls=%fused_computation.40 | convolution fusion | flops 12582912 | bytes 1572864 | tf_op jit(solution)/shard_map/aghd,bghd->ghab/dot_general | solution.py:152
  62.5 8.2 %fusion.15 = f32[24,8,32,32]{3,2,1,0:T(8,128)} fusion(bf16[32,24,8,32]{0,3,2,1:T(8,128)(2,1)S(1)} %bitcast.139, f32[24,8,32,32]{2,3,1,0:T(8,128)} %fusion.22, f32[24,8,32,32]{2,3,1,0:T(8,128)} %copy-done.5, f32[24,8,32]{2,1,0:T(8,128)S(1)} %get-tuple-element.40, pred[32,32]{0,1:T(8,128)(4,1)S(1)} %fusion.44), kind=kOutput, calls=%fused_computation.31 | convolution fusion | flops 15144991 | bytes 2778112 | tf_op jit(solution)/shard_map/ghab,bghd->aghd/dot_general | solution.py:161
  70.7 6.7 %multiply_convert_fusion = bf16[24,8,32,32]{2,3,1,0:T(8,128)(2,1)S(1)} fusion(f32[24,8,32,32]{2,3,1,0:T(8,128)} %fusion.22, f32[24,8,32]{2,1,0:T(8,128)} %copy-done.17, f32[24,8,32,32]{2,3,1,0:T(8,128)} %copy-done.5, pred[32,32]{0,1:T(8,128)(4,1)S(1)} %fusion.44), kind=kOutput, calls=%fused_computation.5 | output fusion | flops 2168863 | bytes 1991680 | tf_op jit(solution)/shard_map/sub | solution.py:157
  77.4 4.5 %convert_reduce_fusion = f32[24,8,32,32]{3,2,1,0:T(8,128)} fusion(bf16[4,8,24,8,32]{4,3,2,1,0:T(8,128)(2,1)S(1)} %copy-done.7, bf16[24,8,32,32]{3,2,1,0:T(8,128)(2,1)S(1)} %copy-done.8), kind=kOutput, calls=%fused_computation.3 | convolution fusion | flops 14745600 | bytes 1572864 | tf_op jit(solution)/shard_map/ghnyb,nyghd->nbghd/dot_general | solution.py:173
  82.0 2.3 copy.122
  84.3 1.6 copy.91
  85.8 2.3 copy.104
  88.2 6.2 %convert_reduce_fusion.1 = f32[24,8,32,32]{3,2,1,0:T(8,128)} fusion(bf16[4,8,24,8,32]{4,3,2,1,0:T(8,128)(2,1)} %reshape_reshape.8, bf16[24,8,32,32]{3,2,1,0:T(8,128)(2,1)} %copy.91), kind=kOutput, calls=%fused_computation.4 | convolution fusion | flops 14745600 | bytes 1572864 | tf_op jit(solution)/shard_map/ghnyb,nyghd->nbghd/dot_general | solution.py:170
  94.3 2.3 copy.121
  96.6 1.2 subtract_convert_fusion
  99.9 3.8 %copy.108 = bf16[32,24,8,32]{3,2,1,0:T(8,128)(2,1)S(1)} copy(bf16[32,24,8,32]{0,3,2,1:T(8,128)(2,1)} %fusion.26) | data formatting | bytes 786432 | tf_op jit(solution)/shard_map/convert_element_type | solution.py:135
  103.7 1.8 broadcast_in_dim.105
  105.5 2.8 %fusion.12 = f32[2,2,256,768]{2,3,1,0:T(8,128)S(1)} fusion(bf16[1,32,24,768]{3,1,2,0:T(8,128)(2,1)S(1)} %copy-done.14, bf16[1,32,24,768]{3,1,2,0:T(8,128)(2,1)} %fusion.16, pred[2,32]{1,0:T(4,128)(4,1)S(1)} %copy-done.21, bf16[32,24,256]{2,0,1:T(8,128)(2,1)} %copy.105), kind=kOutput, calls=%fused_computation.26 | convolution fusion | flops 1213071360 | bytes 5898304 | tf_op jit(solution)/shard_map/tpc,spe->stce/dot_general | solution.py:190
  110.3 2.4 %copy.110 = f32[2,256,1024]{2,0,1:T(2,128)} copy(f32[2,256,1024]{1,2,0:T(8,128)S(1)} %pad_maximum_fusion.1) | data formatting | bytes 4194304 | tf_op jit(solution)/shard_map/concatenate | solution.py:195
  112.7 2.4 %fusion.62 = (f32[2,2,2,2,2,1,2,4,1024]{8,6,7,5,4,3,2,1,0:T(2,128)S(1)}, f32[2,2,2,2,2,1,2,4,1024]{8,6,7,5,4,3,2,1,0:T(2,128)S(1)}) fusion(f32[2,2,2,2,2,2,2,4,1024]{8,6,7,5,4,3,2,1,0:T(2,128)} %bitcast.127), kind=kLoop, calls=%fused_computation.119 | loop fusion | bytes 4194304 | tf_op jit(solution)/shard_map/slice | solution.py:38
  117.0 2.8 %collective-permute-done.4 = f32[2,2,2,2,2,1,2,4,1024]{8,7,6,5,4,3,2,1,0:T(4,128)} collective-permute-done((f32[2,2,2,2,2,1,2,4,1024]{8,7,6,5,4,3,2,1,0:T(4,128)S(1)}, f32[2,2,2,2,2,1,2,4,1024]{8,7,6,5,4,3,2,1,0:T(4,128)}, u32[]{:S(2)}, u32[]{:S(2)}) %collective-permute-start.4) | collective-permute-done | bytes 1048608 | tf_op jit(solution)/shard_map/ppermute | solution.py:41
  119.8 2.6 %select_add_fusion = f32[2,2,2,2,2,1,2,4,1024]{8,7,6,5,4,3,2,1,0:T(4,128)S(1)} fusion(f32[2,2,2,2,2,1,2,4,1024]{8,7,6,5,4,3,2,1,0:T(4,128)} %collective-permute-done.4, f32[2,2,2,2,2,1,2,4,1024]{8,6,7,5,4,3,2,1,0:T(2,128)} %copy-done.2, f32[2,2,2,2,2,1,2,4,1024]{8,6,7,5,4,3,2,1,0:T(2,128)S(1)} %get-tuple-element.18, pred[]{:T(512)S(6)} %eq.62), kind=kLoop, calls=%fused_computation.50 | loop fusion | flops 524288 | bytes 4194305 | tf_op jit(solution)/shard_map/add | solution.py:41
  123.9 5.1 %copy.90 = f32[32,24,8,32]{3,2,1,0:T(8,128)} copy(f32[32,24,8,32]{0,3,2,1:T(8,128)} %bitcast.124) | data formatting | bytes 1572864 | tf_op jit(solution)/shard_map/concatenate | solution.py:178
  129.0 2.4 %reshape.324 = f32[1,768,256]{2,1,0:T(8,128)S(1)} reshape(f32[32,24,8,32]{3,2,1,0:T(8,128)} %copy.90) | data formatting | bytes 1572864 | tf_op jit(solution)/shard_map/concatenate | solution.py:178
  131.4 4.8 %copy.94 = f32[32,24,8,32]{3,2,1,0:T(8,128)} copy(f32[32,24,8,32]{0,3,2,1:T(8,128)} %bitcast.126) | data formatting | bytes 1572864 | tf_op jit(solution)/shard_map/reduce_sum | solution.py:176
  136.2 2.4 %concatenate.75 = f32[1,768,256]{2,1,0:T(8,128)S(1)} reshape(f32[32,24,8,32]{3,2,1,0:T(8,128)} %copy.94) | data formatting | bytes 1572864 | tf_op jit(solution)/shard_map/concatenate | solution.py:178
  138.6 4.8 %copy.100 = f32[32,24,8,32]{3,2,1,0:T(8,128)} copy(f32[32,24,8,32]{0,3,2,1:T(8,128)} %bitcast.122) | data formatting | bytes 1572864 | tf_op jit(solution)/shard_map/reduce_sum | solution.py:177
  143.4 3.1 %concatenate.76 = f32[1,768,256]{2,1,0:T(8,128)} reshape(f32[32,24,8,32]{3,2,1,0:T(8,128)} %copy.100) | data formatting | bytes 1572864 | tf_op jit(solution)/shard_map/concatenate | solution.py:178
  147.7 1.3 select_add_fusion.1
  150.0 7.5 %collective-permute-done.6 = f32[2,1,2,2,1,1,2,4,1024]{8,7,6,5,4,3,2,1,0:T(4,128)S(1)} collective-permute-done((f32[2,1,2,2,1,1,2,4,1024]{8,7,6,5,4,3,2,1,0:T(4,128)S(1)}, f32[2,1,2,2,1,1,2,4,1024]{8,7,6,5,4,3,2,1,0:T(4,128)S(1)}, u32[]{:S(2)}, u32[]{:S(2)}) %collective-permute-start.6) | collective-permute-done | bytes 262176 | tf_op jit(solution)/shard_map/ppermute | solution.py:41
  157.7 5.8 %collective-permute-start.7 = (f32[2,1,2,1,1,1,2,4,1024]{8,7,6,5,4,3,2,1,0:T(4,128)S(1)}, f32[2,1,2,1,1,1,2,4,1024]{8,7,6,5,4,3,2,1,0:T(4,128)S(1)}, u32[]{:S(2)}, u32[]{:S(2)}) collective-permute-start(f32[2,1,2,1,1,1,2,4,1024]{8,7,6,5,4,3,2,1,0:T(4,128)S(1)} %slice_select_fusion.2), channel_id=1, source_target_pairs={{0,4},{1,5},{2,6},{3,7},{4,0},{5,1},{6,2},{7,3},{8,12},{9,13},{10,... | collective-permute-start | bytes 393224 | tf_op jit(solution)/shard_map/ppermute | solution.py:41
  163.4 1.4 fusion.13
  164.9 4.3 %collective-permute-done.7 = f32[2,1,2,1,1,1,2,4,1024]{8,7,6,5,4,3,2,1,0:T(4,128)S(1)} collective-permute-done((f32[2,1,2,1,1,1,2,4,1024]{8,7,6,5,4,3,2,1,0:T(4,128)S(1)}, f32[2,1,2,1,1,1,2,4,1024]{8,7,6,5,4,3,2,1,0:T(4,128)S(1)}, u32[]{:S(2)}, u32[]{:S(2)}) %collective-permute-start.7) | collective-permute-done | bytes 131104 | tf_op jit(solution)/shard_map/ppermute | solution.py:41
  169.2 2.2 collective-permute-start.8
  171.6 3.5 %collective-permute-done.8 = f32[1,1,2,1,1,1,2,4,1024]{8,7,6,5,4,3,2,1,0:T(4,128)S(1)} collective-permute-done((f32[1,1,2,1,1,1,2,4,1024]{8,7,6,5,4,3,2,1,0:T(4,128)S(1)}, f32[1,1,2,1,1,1,2,4,1024]{8,7,6,5,4,3,2,1,0:T(4,128)S(1)}, u32[]{:S(2)}, u32[]{:S(2)}) %collective-permute-start.8) | collective-permute-done | bytes 65568 | tf_op jit(solution)/shard_map/ppermute | solution.py:41
  175.1 2.4 %collective-permute-start.9 = (f32[1,1,1,1,1,1,2,4,1024]{8,7,6,5,4,3,2,1,0:T(4,128)S(1)}, f32[1,1,1,1,1,1,2,4,1024]{8,7,6,5,4,3,2,1,0:T(4,128)S(1)}, u32[]{:S(2)}, u32[]{:S(2)}) collective-permute-start(f32[1,1,1,1,1,1,2,4,1024]{8,7,6,5,4,3,2,1,0:T(4,128)S(1)} %slice_select_fusion.4), channel_id=1, source_target_pairs={{0,8},{1,9},{2,10},{3,11},{4,12},{5,13},{6,14},{7,15},{8,0},{9,1},... | collective-permute-start | bytes 98312 | tf_op jit(solution)/shard_map/ppermute | solution.py:41
  177.6 5.4 %collective-permute-done.9 = f32[1,1,1,1,1,1,2,4,1024]{8,7,6,5,4,3,2,1,0:T(4,128)S(1)} collective-permute-done((f32[1,1,1,1,1,1,2,4,1024]{8,7,6,5,4,3,2,1,0:T(4,128)S(1)}, f32[1,1,1,1,1,1,2,4,1024]{8,7,6,5,4,3,2,1,0:T(4,128)S(1)}, u32[]{:S(2)}, u32[]{:S(2)}) %collective-permute-start.9) | collective-permute-done | bytes 32800 | tf_op jit(solution)/shard_map/ppermute | solution.py:41
  183.1 1.8 collective-permute-start.10
  185.8 3.9 %all-to-all-start.2 = ((bf16[32,24,256]{2,1,0:T(8,128)(2,1)}), bf16[32,24,256]{2,1,0:T(8,128)(2,1)S(1)}, u32[]{:S(2)}, u32[]{:S(2)}) async-start(bf16[32,24,256]{2,1,0:T(8,128)(2,1)} %select_convert_fusion), calls=%async_computation.2 | async-start | bytes 786432 | tf_op jit(solution)/shard_map/all_to_all | solution.py:185
  189.7 3.6 %collective-permute-start.11 = (f32[2,4,1024]{2,1,0:T(4,128)S(1)}, f32[2,4,1024]{2,1,0:T(4,128)S(1)}, u32[]{:S(2)}, u32[]{:S(2)}) collective-permute-start(f32[2,4,1024]{2,1,0:T(4,128)S(1)} %add.123), channel_id=1, source_target_pairs={{0,128},{64,192},{128,0},{192,64},{1,129},{65,193},{129,1},{193,65... | collective-permute-start | bytes 98312 | tf_op jit(solution)/shard_map/ppermute | solution.py:48
  193.3 4.1 %collective-permute-done.11 = f32[2,4,1024]{2,1,0:T(4,128)S(1)} collective-permute-done((f32[2,4,1024]{2,1,0:T(4,128)S(1)}, f32[2,4,1024]{2,1,0:T(4,128)S(1)}, u32[]{:S(2)}, u32[]{:S(2)}) %collective-permute-start.11) | collective-permute-done | bytes 32800 | tf_op jit(solution)/shard_map/ppermute | solution.py:48
  200.9 2.1 collective-permute-start.2
  203.0 5.6 %collective-permute-start.3 = (bf16[8,2,24,256]{3,0,2,1:T(8,128)(2,1)S(1)}, bf16[8,2,24,256]{3,0,2,1:T(8,128)(2,1)S(1)}, u32[]{:S(2)}, u32[]{:S(2)}) collective-permute-start(bf16[8,2,24,256]{3,0,2,1:T(8,128)(2,1)S(1)} %get-tuple-element.28), channel_id=1, source_target_pairs={{1,0},{2,1},{3,2},{4,3},{5,4},{6,5},{7,6},{8,7},{9,8},{10,9},{11,1... | collective-permute-start | bytes 589832 | tf_op jit(solution)/shard_map/ppermute | solution.py:62
  210.5 3.4 %collective-permute-done.14 = f32[8,128]{1,0:T(8,128)S(1)} collective-permute-done((f32[8,128]{1,0:T(8,128)S(1)}, f32[8,128]{1,0:T(8,128)S(1)}, u32[]{:S(2)}, u32[]{:S(2)}) %collective-permute-start.14) | collective-permute-done | bytes 4128 | tf_op jit(solution)/shard_map/ppermute | solution.py:48
  213.9 1.4 collective-permute-start.15
  215.3 6.1 %collective-permute-done.15 = f32[8,128]{1,0:T(8,128)S(1)} collective-permute-done((f32[8,128]{1,0:T(8,128)S(1)}, f32[8,128]{1,0:T(8,128)S(1)}, u32[]{:S(2)}, u32[]{:S(2)}) %collective-permute-start.15) | collective-permute-done | bytes 4128 | tf_op jit(solution)/shard_map/ppermute | solution.py:48
  221.5 3.5 %collective-permute-done.16 = f32[8,128]{1,0:T(8,128)S(1)} collective-permute-done((f32[8,128]{1,0:T(8,128)S(1)}, f32[8,128]{1,0:T(8,128)S(1)}, u32[]{:S(2)}, u32[]{:S(2)}) %collective-permute-start.16) | collective-permute-done | bytes 4128 | tf_op jit(solution)/shard_map/ppermute | solution.py:48
  225.0 2.1 collective-permute-start.17
  227.2 1.7 gather_fusion.1
  (131 shorter events, 26.8 us)
Async XLA Ops:
  0.6 40.2 %copy-start = (bf16[2,256,768]{2,1,0:T(8,128)(2,1)S(1)}, bf16[2,256,768]{2,1,0:T(8,128)(2,1)}, u32[]{:S(2)}) copy-start(bf16[2,256,768]{2,1,0:T(8,128)(2,1)} %param.11) | copy-start | bytes 2359300
  0.6 16.6 %copy-start.23 = (s32[32]{0:T(128)S(1)}, s32[32]{0:T(128)}, u32[]{:S(2)}) copy-start(s32[32]{0:T(128)} %param.9) | copy-start | bytes 388
  0.7 16.6 %copy-start.22 = (s32[32]{0:T(128)S(1)}, s32[32]{0:T(128)}, u32[]{:S(2)}) copy-start(s32[32]{0:T(128)} %param.8) | copy-start | bytes 388
  0.7 17.5 %copy-start.18 = (s32[32,2]{0,1:T(2,128)S(1)}, s32[32,2]{0,1:T(2,128)}, u32[]{:S(2)}) copy-start(s32[32,2]{0,1:T(2,128)} %param.10) | copy-start | bytes 772
  2.7 20.4 %all-to-all-start.1 = ((bf16[8,96,256]{2,0,1:T(8,128)(2,1)}), bf16[8,96,256]{2,0,1:T(8,128)(2,1)S(1)}, u32[]{:S(2)}, u32[]{:S(2)}) async-start(bf16[8,96,256]{2,0,1:T(8,128)(2,1)} %bitcast.11), calls=%async_computation.1 | async-start | bytes 786432 | tf_op jit(solution)/shard_map/all_to_all | solution.py:107
  8.4 10.2 %collective-permute-start = (bf16[8,2,24,256]{3,0,2,1:T(8,128)(2,1)S(1)}, bf16[8,2,24,256]{3,0,2,1:T(8,128)(2,1)S(1)}, u32[]{:S(2)}, u32[]{:S(2)}) collective-permute-start(bf16[8,2,24,256]{3,0,2,1:T(8,128)(2,1)S(1)} %get-tuple-element.33), channel_id=1, source_target_pairs={{0,1},{1,2},{2,3},{3,4},{4,5},{5,6},{6,7},{7,8},{8,9},{9,10},{10,1... | collective-permute-start | bytes 589832 | tf_op jit(solution)/shard_map/ppermute | solution.py:60
  10.3 10.1 %collective-permute-start.1 = (bf16[8,2,24,256]{3,0,2,1:T(8,128)(2,1)S(1)}, bf16[8,2,24,256]{3,0,2,1:T(8,128)(2,1)S(1)}, u32[]{:S(2)}, u32[]{:S(2)}) collective-permute-start(bf16[8,2,24,256]{3,0,2,1:T(8,128)(2,1)S(1)} %get-tuple-element.34), channel_id=1, source_target_pairs={{1,0},{2,1},{3,2},{4,3},{5,4},{6,5},{7,6},{8,7},{9,8},{10,9},{11,1... | collective-permute-start | bytes 589832 | tf_op jit(solution)/shard_map/ppermute | solution.py:62
  18.0 0.7 copy-start.20
  22.2 6.1 %copy-start.16 = (bf16[2,256,256]{2,1,0:T(8,128)(2,1)S(1)}, bf16[2,256,256]{2,1,0:T(8,128)(2,1)}, u32[]{:S(2)}) copy-start(bf16[2,256,256]{2,1,0:T(8,128)(2,1)} %param.12) | copy-start | bytes 786436
  23.1 17.6 %all-to-all-start = ((bf16[4,8,24,256]{3,2,1,0:T(8,128)(2,1)}), bf16[4,8,24,256]{3,2,1,0:T(8,128)(2,1)S(1)}, u32[]{:S(2)}, u32[]{:S(2)}) async-start(bf16[4,8,24,256]{3,2,1,0:T(8,128)(2,1)} %pad_maximum_fusion.2), calls=%async_computation | async-start | bytes 786432 | tf_op jit(solution)/shard_map/all_to_all | solution.py:102
  28.3 1.2 copy-start.9
  29.7 2.5 %copy-start.11 = (bf16[1,768,256]{1,2,0:T(8,128)(2,1)S(1)}, bf16[1,768,256]{1,2,0:T(8,128)(2,1)}, u32[]{:S(2)}) copy-start(bf16[1,768,256]{1,2,0:T(8,128)(2,1)} %get-tuple-element.25) | copy-start | bytes 1179652
  35.9 3.4 %copy-start.4 = (bf16[4,8,24,8,32]{4,3,2,1,0:T(8,128)(2,1)S(1)}, bf16[4,8,24,8,32]{4,3,2,1,0:T(8,128)(2,1)}, u32[]{:S(2)}) copy-start(bf16[4,8,24,8,32]{4,3,2,1,0:T(8,128)(2,1)} %squeeze.36) | copy-start | bytes 1179652
  35.9 3.4 %copy-start.19 = (pred[4,8]{1,0:T(4,128)(4,1)S(1)}, pred[4,8]{1,0:T(4,128)(4,1)}, u32[]{:S(2)}) copy-start(pred[4,8]{1,0:T(4,128)(4,1)} %broadcast_in_dim.96) | copy-start | bytes 100
  48.1 3.8 %copy-start.12 = (bf16[32,24,256]{0,2,1:T(8,128)(2,1)}, bf16[32,24,256]{0,2,1:T(8,128)(2,1)S(1)}, u32[]{:S(2)}) copy-start(bf16[32,24,256]{0,2,1:T(8,128)(2,1)S(1)} %copy.130) | copy-start | bytes 1179652
  52.0 1.7 copy-start.5
  52.0 10.5 %copy-start.17 = (f32[24,8,32]{2,1,0:T(8,128)}, f32[24,8,32]{2,1,0:T(8,128)S(1)}, u32[]{:S(2)}) copy-start(f32[24,8,32]{2,1,0:T(8,128)S(1)} %get-tuple-element.40) | copy-start | bytes 73732
  56.2 3.4 %copy-start.1 = (bf16[32,24,256]{0,2,1:T(8,128)(2,1)S(1)}, bf16[32,24,256]{0,2,1:T(8,128)(2,1)}, u32[]{:S(2)}) copy-start(bf16[32,24,256]{0,2,1:T(8,128)(2,1)} %copy.131) | copy-start | bytes 1179652
  56.2 3.4 %copy-start.3 = (bf16[32,24,8,32]{3,2,1,0:T(8,128)(2,1)S(1)}, bf16[32,24,8,32]{3,2,1,0:T(8,128)(2,1)}, u32[]{:S(2)}) copy-start(bf16[32,24,8,32]{3,2,1,0:T(8,128)(2,1)} %broadcast_select_fusion) | copy-start | bytes 1179652
  59.6 2.9 %copy-start.13 = (bf16[32,24,256]{0,2,1:T(8,128)(2,1)S(1)}, bf16[32,24,256]{0,2,1:T(8,128)(2,1)}, u32[]{:S(2)}) copy-start(bf16[32,24,256]{0,2,1:T(8,128)(2,1)} %copy-done.12) | copy-start | bytes 1179652
  70.7 6.7 %copy-start.7 = (bf16[4,8,24,8,32]{4,3,2,1,0:T(8,128)(2,1)S(1)}, bf16[4,8,24,8,32]{4,3,2,1,0:T(8,128)(2,1)}, u32[]{:S(2)}) copy-start(bf16[4,8,24,8,32]{4,3,2,1,0:T(8,128)(2,1)} %broadcast_select_fusion.1) | copy-start | bytes 1179652
  70.7 6.7 %copy-start.8 = (bf16[24,8,32,32]{3,2,1,0:T(8,128)(2,1)S(1)}, bf16[24,8,32,32]{3,2,1,0:T(8,128)(2,1)}, u32[]{:S(2)}) copy-start(bf16[24,8,32,32]{3,2,1,0:T(8,128)(2,1)} %copy.97) | copy-start | bytes 1179652
  99.9 5.7 %copy-start.14 = (bf16[1,32,24,768]{3,1,2,0:T(8,128)(2,1)S(1)}, bf16[1,32,24,768]{3,1,2,0:T(8,128)(2,1)}, u32[]{:S(2)}) copy-start(bf16[1,32,24,768]{3,1,2,0:T(8,128)(2,1)} %subtract_convert_fusion) | copy-start | bytes 3538948
  99.9 5.7 %copy-start.21 = (pred[2,32]{1,0:T(4,128)(4,1)S(1)}, pred[2,32]{1,0:T(4,128)(4,1)}, u32[]{:S(2)}) copy-start(pred[2,32]{1,0:T(4,128)(4,1)} %copy-done.20) | copy-start | bytes 196
  108.4 1.0 copy-start.10
  108.4 1.1 copy-start.15
  115.1 1.0 copy-start.2
  116.9 2.9 %collective-permute-start.4 = (f32[2,2,2,2,2,1,2,4,1024]{8,7,6,5,4,3,2,1,0:T(4,128)S(1)}, f32[2,2,2,2,2,1,2,4,1024]{8,7,6,5,4,3,2,1,0:T(4,128)}, u32[]{:S(2)}, u32[]{:S(2)}) collective-permute-start(f32[2,2,2,2,2,1,2,4,1024]{8,7,6,5,4,3,2,1,0:T(4,128)S(1)} %copy_select_fusion), channel_id=1, source_target_pairs={{0,1},{1,0},{2,3},{3,2},{4,5},{5,4},{6,7},{7,6},{8,9},{9,8},{10,11... | collective-permute-start | bytes 3145736 | tf_op jit(solution)/shard_map/ppermute | solution.py:41
  123.4 24.4 %collective-permute-start.5 = (f32[2,2,2,2,1,1,2,4,1024]{8,7,6,5,4,3,2,1,0:T(4,128)}, f32[2,2,2,2,1,1,2,4,1024]{8,7,6,5,4,3,2,1,0:T(4,128)}, u32[]{:S(2)}, u32[]{:S(2)}) collective-permute-start(f32[2,2,2,2,1,1,2,4,1024]{8,7,6,5,4,3,2,1,0:T(4,128)} %slice_select_fusion), channel_id=1, source_target_pairs={{0,2},{1,3},{2,0},{3,1},{4,6},{5,7},{6,4},{7,5},{8,10},{9,11},{10,... | collective-permute-start | bytes 1572872 | tf_op jit(solution)/shard_map/ppermute | solution.py:41
  146.5 1.1 copy-start.6
  149.1 8.4 %collective-permute-start.6 = (f32[2,1,2,2,1,1,2,4,1024]{8,7,6,5,4,3,2,1,0:T(4,128)S(1)}, f32[2,1,2,2,1,1,2,4,1024]{8,7,6,5,4,3,2,1,0:T(4,128)S(1)}, u32[]{:S(2)}, u32[]{:S(2)}) collective-permute-start(f32[2,1,2,2,1,1,2,4,1024]{8,7,6,5,4,3,2,1,0:T(4,128)S(1)} %slice_select_fusion.1), channel_id=1, source_target_pairs={{0,16},{1,17},{2,18},{3,19},{4,20},{5,21},{6,22},{7,23},{8,24},{9,... | collective-permute-start | bytes 786440 | tf_op jit(solution)/shard_map/ppermute | solution.py:41
  157.7 11.5 %collective-permute-start.7 = (f32[2,1,2,1,1,1,2,4,1024]{8,7,6,5,4,3,2,1,0:T(4,128)S(1)}, f32[2,1,2,1,1,1,2,4,1024]{8,7,6,5,4,3,2,1,0:T(4,128)S(1)}, u32[]{:S(2)}, u32[]{:S(2)}) collective-permute-start(f32[2,1,2,1,1,1,2,4,1024]{8,7,6,5,4,3,2,1,0:T(4,128)S(1)} %slice_select_fusion.2), channel_id=1, source_target_pairs={{0,4},{1,5},{2,6},{3,7},{4,0},{5,1},{6,2},{7,3},{8,12},{9,13},{10,... | collective-permute-start | bytes 393224 | tf_op jit(solution)/shard_map/ppermute | solution.py:41
  169.2 5.9 %collective-permute-start.8 = (f32[1,1,2,1,1,1,2,4,1024]{8,7,6,5,4,3,2,1,0:T(4,128)S(1)}, f32[1,1,2,1,1,1,2,4,1024]{8,7,6,5,4,3,2,1,0:T(4,128)S(1)}, u32[]{:S(2)}, u32[]{:S(2)}) collective-permute-start(f32[1,1,2,1,1,1,2,4,1024]{8,7,6,5,4,3,2,1,0:T(4,128)S(1)} %slice_select_fusion.3), channel_id=1, source_target_pairs={{0,32},{1,33},{2,34},{3,35},{4,36},{5,37},{6,38},{7,39},{8,40},{9,... | collective-permute-start | bytes 196616 | tf_op jit(solution)/shard_map/ppermute | solution.py:41
  175.1 7.9 %collective-permute-start.9 = (f32[1,1,1,1,1,1,2,4,1024]{8,7,6,5,4,3,2,1,0:T(4,128)S(1)}, f32[1,1,1,1,1,1,2,4,1024]{8,7,6,5,4,3,2,1,0:T(4,128)S(1)}, u32[]{:S(2)}, u32[]{:S(2)}) collective-permute-start(f32[1,1,1,1,1,1,2,4,1024]{8,7,6,5,4,3,2,1,0:T(4,128)S(1)} %slice_select_fusion.4), channel_id=1, source_target_pairs={{0,8},{1,9},{2,10},{3,11},{4,12},{5,13},{6,14},{7,15},{8,0},{9,1},... | collective-permute-start | bytes 98312 | tf_op jit(solution)/shard_map/ppermute | solution.py:41
  183.1 6.6 %collective-permute-start.10 = (f32[2,4,1024]{2,1,0:T(4,128)S(1)}, f32[2,4,1024]{2,1,0:T(4,128)S(1)}, u32[]{:S(2)}, u32[]{:S(2)}) collective-permute-start(f32[2,4,1024]{2,1,0:T(4,128)S(1)} %add_bitcast_fusion), channel_id=1, source_target_pairs={{0,64},{64,0},{128,192},{192,128},{1,65},{65,1},{129,193},{193,129... | collective-permute-start | bytes 98312 | tf_op jit(solution)/shard_map/ppermute | solution.py:48
  185.8 13.2 %all-to-all-start.2 = ((bf16[32,24,256]{2,1,0:T(8,128)(2,1)}), bf16[32,24,256]{2,1,0:T(8,128)(2,1)S(1)}, u32[]{:S(2)}, u32[]{:S(2)}) async-start(bf16[32,24,256]{2,1,0:T(8,128)(2,1)} %select_convert_fusion), calls=%async_computation.2 | async-start | bytes 786432 | tf_op jit(solution)/shard_map/all_to_all | solution.py:185
  189.7 7.7 %collective-permute-start.11 = (f32[2,4,1024]{2,1,0:T(4,128)S(1)}, f32[2,4,1024]{2,1,0:T(4,128)S(1)}, u32[]{:S(2)}, u32[]{:S(2)}) collective-permute-start(f32[2,4,1024]{2,1,0:T(4,128)S(1)} %add.123), channel_id=1, source_target_pairs={{0,128},{64,192},{128,0},{192,64},{1,129},{65,193},{129,1},{193,65... | collective-permute-start | bytes 98312 | tf_op jit(solution)/shard_map/ppermute | solution.py:48
  198.7 1.4 collective-permute-start.12
  200.8 7.8 %collective-permute-start.13 = (f32[8,128]{1,0:T(8,128)S(1)}, f32[8,128]{1,0:T(8,128)S(1)}, u32[]{:S(2)}, u32[]{:S(2)}) collective-permute-start(f32[8,128]{1,0:T(8,128)S(1)} %broadcast_add_fusion), channel_id=1, source_target_pairs={{0,2},{1,3},{2,0},{3,1},{4,6},{5,7},{6,4},{7,5},{8,10},{9,11},{10,... | collective-permute-start | bytes 12296 | tf_op jit(solution)/shard_map/ppermute | solution.py:48
  200.9 26.2 %collective-permute-start.2 = (bf16[8,2,24,256]{3,0,2,1:T(8,128)(2,1)S(1)}, bf16[8,2,24,256]{3,0,2,1:T(8,128)(2,1)S(1)}, u32[]{:S(2)}, u32[]{:S(2)}) collective-permute-start(bf16[8,2,24,256]{3,0,2,1:T(8,128)(2,1)S(1)} %get-tuple-element.27), channel_id=1, source_target_pairs={{0,1},{1,2},{2,3},{3,4},{4,5},{5,6},{6,7},{7,8},{8,9},{9,10},{10,1... | collective-permute-start | bytes 589832 | tf_op jit(solution)/shard_map/ppermute | solution.py:60
  203.0 24.1 %collective-permute-start.3 = (bf16[8,2,24,256]{3,0,2,1:T(8,128)(2,1)S(1)}, bf16[8,2,24,256]{3,0,2,1:T(8,128)(2,1)S(1)}, u32[]{:S(2)}, u32[]{:S(2)}) collective-permute-start(bf16[8,2,24,256]{3,0,2,1:T(8,128)(2,1)S(1)} %get-tuple-element.28), channel_id=1, source_target_pairs={{1,0},{2,1},{3,2},{4,3},{5,4},{6,5},{7,6},{8,7},{9,8},{10,9},{11,1... | collective-permute-start | bytes 589832 | tf_op jit(solution)/shard_map/ppermute | solution.py:62
  209.3 4.6 %collective-permute-start.14 = (f32[8,128]{1,0:T(8,128)S(1)}, f32[8,128]{1,0:T(8,128)S(1)}, u32[]{:S(2)}, u32[]{:S(2)}) collective-permute-start(f32[8,128]{1,0:T(8,128)S(1)} %fusion.79), channel_id=1, source_target_pairs={{0,4},{1,5},{2,6},{3,7},{4,0},{5,1},{6,2},{7,3},{8,12},{9,13},{10,... | collective-permute-start | bytes 12296 | tf_op jit(solution)/shard_map/ppermute | solution.py:48
  213.9 7.5 %collective-permute-start.15 = (f32[8,128]{1,0:T(8,128)S(1)}, f32[8,128]{1,0:T(8,128)S(1)}, u32[]{:S(2)}, u32[]{:S(2)}) collective-permute-start(f32[8,128]{1,0:T(8,128)S(1)} %add.127), channel_id=1, source_target_pairs={{0,8},{1,9},{2,10},{3,11},{4,12},{5,13},{6,14},{7,15},{8,0},{9,1},... | collective-permute-start | bytes 12296 | tf_op jit(solution)/shard_map/ppermute | solution.py:48
  221.4 3.6 %collective-permute-start.16 = (f32[8,128]{1,0:T(8,128)S(1)}, f32[8,128]{1,0:T(8,128)S(1)}, u32[]{:S(2)}, u32[]{:S(2)}) collective-permute-start(f32[8,128]{1,0:T(8,128)S(1)} %add.128), channel_id=1, source_target_pairs={{0,16},{1,17},{2,18},{3,19},{4,20},{5,21},{6,22},{7,23},{8,24},{9,... | collective-permute-start | bytes 12296 | tf_op jit(solution)/shard_map/ppermute | solution.py:48
  225.0 5.1 %collective-permute-start.17 = (f32[8,128]{1,0:T(8,128)S(1)}, f32[8,128]{1,0:T(8,128)S(1)}, u32[]{:S(2)}, u32[]{:S(2)}) collective-permute-start(f32[8,128]{1,0:T(8,128)S(1)} %add.129), channel_id=1, source_target_pairs={{0,32},{1,33},{2,34},{3,35},{4,36},{5,37},{6,38},{7,39},{8,40},{9,... | collective-permute-start | bytes 12296 | tf_op jit(solution)/shard_map/ppermute | solution.py:48
